TPU v7x, 32 devices: a whole 2x2x4 slice. The times are simulated.
32 devices in a mesh: groups: 2 (over y), section: 4 (over x, core), filt: 4 (over z).
Axes of the slice: x: 2, y: 2, z: 4, core: 2. Of those that a mesh axis runs over, the one named last changes fastest.
Arguments:
- volumes: bfloat16 [16, 256, 4, 2, 128], P('groups', 'filt'), parts along dimension 0, may hold values from -6 to 6
- weights: bfloat16 [4, 256, 27, 256], P('section', 'filt'), may hold values from -0.125 to 0.125
- biases: float32 [4, 256], P('section', 'filt'), may hold values from -3 to 3
- cotangent: bfloat16 [16, 256, 4, 2, 128], P('groups', 'filt'), parts along dimension 0, may hold values from -6 to 6
Outputs:
- grad_weights: float32 [8, 256, 27, 256], P(('groups', 'section'), 'filt'), parts along dimension 0
- grad_biases: float32 [8, 256], P(('groups', 'section'), 'filt'), parts along dimension 0
- grad_inputs: bfloat16 [8, 8, 256, 4, 2, 128], P(('groups', 'section'), None, 'filt'), parts along dimension 0
There are 2 independent parts, one for each index of `groups`. A program takes and returns all parts, laid end to end along the dimension named above; an argument that names none is the same for every part. Nothing has to cross between parts.
All inputs are finite; a program needn't handle non-finite values.
Results may differ from a plain program's by a relative error of at most 0.019.
Values may be sent and summed in bfloat16 or wider, within the bound.
No kernel may reach another device: no remote copies, remote signals or barrier semaphores. Data moves between devices by JAX's collectives and lax.ppermute only.
A program may use at most 64 MiB of HBM per device.

v0:
```python
import math
import jax
import jax.numpy as jnp
from jax import lax
from jax.sharding import PartitionSpec as P

CHUNK = 1
PAD3 = ((1, 1), (1, 1), (1, 1))


def silu_slope(pre_act):
    sigmoid = jax.nn.sigmoid(pre_act)
    return sigmoid * (1.0 + pre_act * (1.0 - sigmoid))


def conv_forward(act, kernel):
    return lax.conv_general_dilated(
        act,
        kernel,
        (1, 1, 1),
        PAD3,
        dimension_numbers=("NCDHW", "ODHWI", "NCDHW"),
        preferred_element_type=jnp.float32,
    )


def conv_input_grad(slope, kernel):
    flipped = kernel[:, ::-1, ::-1, ::-1, :]
    return lax.conv_general_dilated(
        slope,
        flipped,
        (1, 1, 1),
        PAD3,
        dimension_numbers=("NCDHW", "IDHWO", "NCDHW"),
        preferred_element_type=jnp.float32,
    )


def conv_weight_grad(act, slope):
    return lax.conv_general_dilated(
        act,
        slope,
        (1, 1, 1),
        PAD3,
        dimension_numbers=("CNDHW", "IODHW", "CDHWN"),
        preferred_element_type=jnp.float32,
    )


def local(volumes, weights, biases, cotangent):
    section_count = lax.axis_size("section")
    section_pos = lax.axis_index("section")
    micro_count = volumes.shape[0]
    chunk = CHUNK if micro_count % CHUNK == 0 else 1
    chunk_count = micro_count // chunk
    tick_count = chunk_count + section_count - 1
    own_count, tap_count, channels = weights.shape[1:]
    extent = volumes.shape[2:]
    kernel = weights[0].reshape(own_count, 3, 3, 3, channels)
    layer_bias = biases[0][None, :, None, None, None]
    slab = (chunk, own_count) + tuple(extent)
    forward_pairs = [(i, i + 1) for i in range(section_count - 1)]
    backward_pairs = [(i + 1, i) for i in range(section_count - 1)]
    incoming = jnp.zeros(slab, jnp.bfloat16)
    gathered = []
    pres = []
    for tick in range(tick_count):
        if tick < chunk_count:
            first = volumes[tick * chunk : (tick + 1) * chunk]
        else:
            first = jnp.zeros(slab, jnp.bfloat16)
        own_input = jnp.where(section_pos == 0, first, incoming)
        full_input = lax.all_gather(own_input, "filt", axis=1, tiled=True)
        pre_act = conv_forward(full_input, kernel) + layer_bias
        gathered.append(full_input)
        pres.append(pre_act)
        if tick < tick_count - 1:
            outgoing = jax.nn.silu(pre_act).astype(jnp.bfloat16)
            incoming = lax.ppermute(outgoing, "section", forward_pairs)
    incoming = jnp.zeros(slab, jnp.bfloat16)
    grad_kernel = jnp.zeros((own_count, 3, 3, 3, channels), jnp.float32)
    grad_bias = jnp.zeros((own_count,), jnp.float32)
    results = []
    for tick in range(tick_count):
        forward_tick = tick_count - 1 - tick
        if tick < chunk_count:
            start = (chunk_count - 1 - tick) * chunk
            last = cotangent[start : start + chunk]
        else:
            last = jnp.zeros(slab, jnp.bfloat16)
        upstream = jnp.where(section_pos == section_count - 1, last, incoming)
        sample = forward_tick - section_pos
        in_range = (sample >= 0) & (sample < chunk_count)
        slope = (upstream.astype(jnp.float32) * silu_slope(pres[forward_tick])).astype(jnp.bfloat16)
        slope = jnp.where(in_range, slope, jnp.zeros((), jnp.bfloat16))
        grad_kernel = grad_kernel + conv_weight_grad(gathered[forward_tick], slope)
        grad_bias = grad_bias + jnp.sum(slope.astype(jnp.float32), axis=(0, 2, 3, 4))
        partial = jnp.moveaxis(conv_input_grad(slope, kernel).astype(jnp.bfloat16), 1, 0)
        partial = partial.reshape(channels, chunk * extent[0] * extent[1], extent[2])
        scattered = lax.psum_scatter(partial, "filt", scatter_dimension=0, tiled=True)
        input_grad = jnp.moveaxis(scattered.reshape((own_count, chunk) + tuple(extent)), 0, 1)
        results.append(input_grad)
        if tick < tick_count - 1:
            incoming = lax.ppermute(input_grad, "section", backward_pairs)
    reversed_results = jnp.stack(results[::-1])
    picked = lax.dynamic_slice_in_dim(reversed_results, section_pos, chunk_count, axis=0)
    grad_in = picked.reshape((1, micro_count, own_count) + tuple(extent))
    norm_scale = 1.0 / math.sqrt(micro_count * math.prod(extent))
    return (
        (grad_kernel * norm_scale).reshape(1, own_count, tap_count, channels),
        (grad_bias * norm_scale)[None],
        grad_in,
    )


def solution(mesh):
    in_specs = (
        P("groups", "filt", None, None, None),
        P("section", "filt", None, None),
        P("section", "filt"),
        P("groups", "filt", None, None, None),
    )
    out_specs = (
        P(("groups", "section"), "filt", None, None),
        P(("groups", "section"), "filt"),
        P(("groups", "section"), None, "filt", None, None, None),
    )
    return jax.shard_map(local, mesh=mesh, in_specs=in_specs, out_specs=out_specs, check_vma=False)
```

profile of v0, /device:TPU:1, one launch (start us, length us, event | category | flops | bytes accessed | tf_op | source)
XLA Modules:
  0.0 906.7 jit_solution(9746588383378449853)
XLA Ops:
  10.6 15.3 %all_gather.33 = bf16[1,256,4,2,128]{4,2,3,0,1:T(4,128)(2,1)S(1)} all-gather(bf16[1,64,4,2,128]{4,2,3,0,1:T(4,128)(2,1)S(1)} %copy.410), channel_id=1, replica_groups=mesh['groups'=2,'section'=4,'filt'=4] {'filt'}, dimensions={1}, use_global_device_ids=true | all-gather | bytes 655360 | tf_op jit(solution)/shard_map/all_gather | solution.py:73
  41.1 13.3 %all_gather.34 = bf16[1,256,4,2,128]{4,2,3,0,1:T(4,128)(2,1)S(1)} all-gather(bf16[1,64,4,2,128]{4,2,3,0,1:T(4,128)(2,1)S(1)} %copy.416), channel_id=1, replica_groups=mesh['groups'=2,'section'=4,'filt'=4] {'filt'}, dimensions={1}, use_global_device_ids=true | all-gather | bytes 655360 | tf_op jit(solution)/shard_map/all_gather | solution.py:73
  60.8 7.4 collective-permute-start.1
  71.6 13.6 %all_gather.35 = bf16[1,256,4,2,128]{4,2,3,0,1:T(4,128)(2,1)S(1)} all-gather(bf16[1,64,4,2,128]{4,2,3,0,1:T(4,128)(2,1)S(1)} %copy.422), channel_id=1, replica_groups=mesh['groups'=2,'section'=4,'filt'=4] {'filt'}, dimensions={1}, use_global_device_ids=true | all-gather | bytes 655360 | tf_op jit(solution)/shard_map/all_gather | solution.py:73
  101.7 13.5 %all_gather.36 = bf16[1,256,4,2,128]{4,2,3,0,1:T(4,128)(2,1)S(1)} all-gather(bf16[1,64,4,2,128]{4,2,3,0,1:T(4,128)(2,1)S(1)} %copy.428), channel_id=1, replica_groups=mesh['groups'=2,'section'=4,'filt'=4] {'filt'}, dimensions={1}, use_global_device_ids=true | all-gather | bytes 655360 | tf_op jit(solution)/shard_map/all_gather | solution.py:73
  124.0 6.8 collective-permute-start.3
  136.2 13.4 %all_gather.37 = bf16[1,256,4,2,128]{4,2,3,0,1:T(4,128)(2,1)S(1)} all-gather(bf16[1,64,4,2,128]{4,2,3,0,1:T(4,128)(2,1)} %copy.434), channel_id=1, replica_groups=mesh['groups'=2,'section'=4,'filt'=4] {'filt'}, dimensions={1}, use_global_device_ids=true | all-gather | bytes 655360 | tf_op jit(solution)/shard_map/all_gather | solution.py:73
  160.2 7.2 collective-permute-start.4
  174.5 14.0 %all_gather.38 = bf16[1,256,4,2,128]{4,2,3,0,1:T(4,128)(2,1)S(1)} all-gather(bf16[1,64,4,2,128]{4,2,3,0,1:T(4,128)(2,1)} %copy.440), channel_id=1, replica_groups=mesh['groups'=2,'section'=4,'filt'=4] {'filt'}, dimensions={1}, use_global_device_ids=true | all-gather | bytes 655360 | tf_op jit(solution)/shard_map/all_gather | solution.py:73
  213.3 13.6 %all_gather.39 = bf16[1,256,4,2,128]{4,2,3,0,1:T(4,128)(2,1)S(1)} all-gather(bf16[1,64,4,2,128]{4,2,3,0,1:T(4,128)(2,1)} %copy.446), channel_id=1, replica_groups=mesh['groups'=2,'section'=4,'filt'=4] {'filt'}, dimensions={1}, use_global_device_ids=true | all-gather | bytes 655360 | tf_op jit(solution)/shard_map/all_gather | solution.py:73
  251.9 13.9 %all_gather.40 = bf16[1,256,4,2,128]{4,2,3,0,1:T(4,128)(2,1)S(1)} all-gather(bf16[1,64,4,2,128]{4,2,3,0,1:T(4,128)(2,1)} %copy.452), channel_id=1, replica_groups=mesh['groups'=2,'section'=4,'filt'=4] {'filt'}, dimensions={1}, use_global_device_ids=true | all-gather | bytes 655360 | tf_op jit(solution)/shard_map/all_gather | solution.py:73
  289.0 13.3 %all_gather.41 = bf16[1,256,4,2,128]{4,2,3,0,1:T(4,128)(2,1)S(1)} all-gather(bf16[1,64,4,2,128]{4,2,3,0,1:T(4,128)(2,1)} %copy.458), channel_id=1, replica_groups=mesh['groups'=2,'section'=4,'filt'=4] {'filt'}, dimensions={1}, use_global_device_ids=true | all-gather | bytes 655360 | tf_op jit(solution)/shard_map/all_gather | solution.py:73
  313.5 7.1 collective-permute-start.8
  328.0 13.1 %all_gather.42 = bf16[1,256,4,2,128]{4,2,3,0,1:T(4,128)(2,1)S(1)} all-gather(bf16[1,64,4,2,128]{4,2,3,0,1:T(4,128)(2,1)} %copy.464), channel_id=1, replica_groups=mesh['groups'=2,'section'=4,'filt'=4] {'filt'}, dimensions={1}, use_global_device_ids=true | all-gather | bytes 655360 | tf_op jit(solution)/shard_map/all_gather | solution.py:73
  352.3 6.8 collective-permute-start.9
  366.4 13.3 %all_gather.43 = bf16[1,256,4,2,128]{4,2,3,0,1:T(4,128)(2,1)S(1)} all-gather(bf16[1,64,4,2,128]{4,2,3,0,1:T(4,128)(2,1)} %copy.470), channel_id=1, replica_groups=mesh['groups'=2,'section'=4,'filt'=4] {'filt'}, dimensions={1}, use_global_device_ids=true | all-gather | bytes 655360 | tf_op jit(solution)/shard_map/all_gather | solution.py:73
  401.5 24.4 %reduce-scatter.12.cloned.1.call-done = bf16[64,8,128]{2,0,1:T(8,128)(2,1)} async-done(((bf16[256,8,128]{2,0,1:T(8,128)(2,1)}), bf16[64,8,128]{2,0,1:T(8,128)(2,1)}) %reduce-scatter.12.cloned.1.call-update) | async-done | bytes 131088 | tf_op jit(solution)/shard_map/reduce_scatter | solution.py:100
  449.8 17.2 %reduce-scatter.14.cloned.1.call-done = bf16[64,8,128]{2,0,1:T(8,128)(2,1)} async-done(((bf16[256,8,128]{2,0,1:T(8,128)(2,1)}), bf16[64,8,128]{2,0,1:T(8,128)(2,1)}) %reduce-scatter.14.cloned.1.call-update) | async-done | bytes 131088 | tf_op jit(solution)/shard_map/reduce_scatter | solution.py:100
  490.7 17.2 %reduce-scatter.16.cloned.1.call-done = bf16[64,8,128]{2,0,1:T(8,128)(2,1)} async-done(((bf16[256,8,128]{2,0,1:T(8,128)(2,1)}), bf16[64,8,128]{2,0,1:T(8,128)(2,1)}) %reduce-scatter.16.cloned.1.call-update) | async-done | bytes 131088 | tf_op jit(solution)/shard_map/reduce_scatter | solution.py:100
  531.7 17.3 %reduce-scatter.18.cloned.1.call-done = bf16[64,8,128]{2,0,1:T(8,128)(2,1)} async-done(((bf16[256,8,128]{2,0,1:T(8,128)(2,1)}), bf16[64,8,128]{2,0,1:T(8,128)(2,1)}) %reduce-scatter.18.cloned.1.call-update) | async-done | bytes 131088 | tf_op jit(solution)/shard_map/reduce_scatter | solution.py:100
  572.3 17.2 %reduce-scatter.20.cloned.1.call-done = bf16[64,8,128]{2,0,1:T(8,128)(2,1)} async-done(((bf16[256,8,128]{2,0,1:T(8,128)(2,1)}), bf16[64,8,128]{2,0,1:T(8,128)(2,1)}) %reduce-scatter.20.cloned.1.call-update) | async-done | bytes 131088 | tf_op jit(solution)/shard_map/reduce_scatter | solution.py:100
  652.1 17.7 %fusion.153 = f32[64,3,3,3,256]{4,0,3,2,1:T(8,128)} fusion(bf16[1,256,4,2,128]{1,0,4,3,2:T(2,128)(2,1)} %copy.477, bf16[1,64,4,2,128]{1,3,4,2,0:T(2,128)(2,1)S(1)} %copy-done.17), kind=kOutput, calls=%fused_computation.241 | convolution fusion | flops 500695040 | bytes 2424832 | tf_op jit(solution)/shard_map/conv_general_dilated | solution.py:40
  674.9 16.8 %fusion.151 = f32[64,3,3,3,256]{4,0,3,2,1:T(8,128)} fusion(bf16[1,256,4,2,128]{1,0,4,3,2:T(2,128)(2,1)S(1)} %copy-done.26, bf16[1,64,4,2,128]{1,3,4,2,0:T(2,128)(2,1)S(1)} %copy-done.28), kind=kOutput, calls=%fused_computation.239 | convolution fusion | flops 500695040 | bytes 2424832 | tf_op jit(solution)/shard_map/conv_general_dilated | solution.py:40
  698.9 16.5 %fusion.149 = f32[64,3,3,3,256]{4,0,3,2,1:T(8,128)} fusion(bf16[1,256,4,2,128]{1,0,4,3,2:T(2,128)(2,1)S(1)} %copy-done.25, bf16[1,64,4,2,128]{1,3,4,2,0:T(2,128)(2,1)S(1)} %copy-done.29), kind=kOutput, calls=%fused_computation.237 | convolution fusion | flops 500695040 | bytes 2424832 | tf_op jit(solution)/shard_map/conv_general_dilated | solution.py:40
  720.6 16.8 %fusion.147 = f32[64,3,3,3,256]{4,0,3,2,1:T(8,128)} fusion(bf16[1,256,4,2,128]{1,0,4,3,2:T(2,128)(2,1)S(1)} %copy-done.24, bf16[1,64,4,2,128]{1,3,4,2,0:T(2,128)(2,1)S(1)} %copy-done.30), kind=kOutput, calls=%fused_computation.235 | convolution fusion | flops 500695040 | bytes 2424832 | tf_op jit(solution)/shard_map/conv_general_dilated | solution.py:40
  744.1 16.6 %fusion.145 = f32[64,3,3,3,256]{4,0,3,2,1:T(8,128)} fusion(bf16[1,256,4,2,128]{1,0,4,3,2:T(2,128)(2,1)S(1)} %copy-done.23, bf16[1,64,4,2,128]{1,3,4,2,0:T(2,128)(2,1)S(1)} %copy-done.31), kind=kOutput, calls=%fused_computation.233 | convolution fusion | flops 500695040 | bytes 2424832 | tf_op jit(solution)/shard_map/conv_general_dilated | solution.py:40
  765.1 18.0 %fusion.143 = f32[64,3,3,3,256]{4,0,3,2,1:T(8,128)} fusion(bf16[1,256,4,2,128]{1,0,4,3,2:T(2,128)(2,1)} %copy.532, bf16[1,64,4,2,128]{1,3,4,2,0:T(2,128)(2,1)S(1)} %copy-done.32), kind=kOutput, calls=%fused_computation.231 | convolution fusion | flops 500695040 | bytes 2424832 | tf_op jit(solution)/shard_map/conv_general_dilated | solution.py:40
  788.7 16.6 %fusion.141 = f32[64,3,3,3,256]{4,0,3,2,1:T(8,128)} fusion(bf16[1,256,4,2,128]{1,0,4,3,2:T(2,128)(2,1)S(1)} %copy-done.22, bf16[1,64,4,2,128]{1,3,4,2,0:T(2,128)(2,1)S(1)} %copy-done.34), kind=kOutput, calls=%fused_computation.229 | convolution fusion | flops 500695040 | bytes 2424832 | tf_op jit(solution)/shard_map/conv_general_dilated | solution.py:40
  809.7 18.0 %fusion.139 = f32[64,3,3,3,256]{4,0,3,2,1:T(8,128)} fusion(bf16[1,256,4,2,128]{1,0,4,3,2:T(2,128)(2,1)} %copy.554, bf16[1,64,4,2,128]{1,3,4,2,0:T(2,128)(2,1)S(1)} %copy-done.36), kind=kOutput, calls=%fused_computation.227 | convolution fusion | flops 500695040 | bytes 2424832 | tf_op jit(solution)/shard_map/conv_general_dilated | solution.py:40
  833.2 16.5 %fusion.137 = f32[64,3,3,3,256]{4,0,3,2,1:T(8,128)} fusion(bf16[1,256,4,2,128]{1,0,4,3,2:T(2,128)(2,1)S(1)} %copy-done.21, bf16[1,64,4,2,128]{1,3,4,2,0:T(2,128)(2,1)S(1)} %get-tuple-element.20), kind=kOutput, calls=%fused_computation.225 | convolution fusion | flops 500695040 | bytes 2424832 | tf_op jit(solution)/shard_map/conv_general_dilated | solution.py:40
  854.1 16.7 %fusion.134 = f32[64,3,3,3,256]{4,0,3,2,1:T(8,128)} fusion(bf16[1,256,4,2,128]{1,0,4,3,2:T(2,128)(2,1)S(1)} %copy-done.19, bf16[1,64,4,2,128]{1,3,4,2,0:T(2,128)(2,1)S(1)} %get-tuple-element.24), kind=kOutput, calls=%fused_computation.222 | convolution fusion | flops 500695040 | bytes 2424832 | tf_op jit(solution)/shard_map/conv_general_dilated | solution.py:40
  870.9 24.5 %add_multiply_fusion = f32[64,3,3,3,256]{4,0,3,2,1:T(8,128)} fusion(f32[64,3,3,3,256]{4,0,3,2,1:T(8,128)} %fusion.134, f32[64,3,3,3,256]{4,0,3,2,1:T(8,128)} %fusion.137, f32[64,3,3,3,256]{4,0,3,2,1:T(8,128)} %fusion.139, f32[64,3,3,3,256]{4,0,3,2,1:T(8,128)} %fusion.141, f32[64,3,3,3,256]{4,0,3,2,1:T(8,128)} %fusion.143, f32[64,3,3,3,256]{4,0,3,2,1:T(8,128)} %fusion.145, ...), kind=kOutput, calls=%fused_computation | convolution fusion | flops 505561088 | bytes 20119552 | tf_op jit(solution)/shard_map/conv_general_dilated | solution.py:40
  (473 shorter events, 416.9 us)
Async XLA Ops:
  7.2 418.7 %reduce-scatter.12.cloned.1.call-start = ((), (), s32[]{:S(2)}) async-start(), calls=%async_computation.11 | async-start | bytes 655360 | tf_op jit(solution)/shard_map/reduce_scatter | solution.py:100
  32.5 8.4 collective-permute-start
  60.8 10.6 %collective-permute-start.1 = (bf16[1,64,4,2,128]{1,3,4,2,0:T(2,128)(2,1)S(1)}, bf16[1,64,4,2,128]{1,3,4,2,0:T(2,128)(2,1)S(1)}, u32[]{:S(2)}, u32[]{:S(2)}) collective-permute-start(bf16[1,64,4,2,128]{1,3,4,2,0:T(2,128)(2,1)S(1)} %slice_bitcast_fusion.30), channel_id=1, source_target_pairs={{0,4},{4,8},{8,12},{1,5},{5,9},{9,13},{2,6},{6,10},{10,14},{3,7},{... | collective-permute-start | bytes 393224 | tf_op jit(solution)/shard_map/ppermute | solution.py:79
  91.6 9.9 %collective-permute-start.2 = (bf16[1,64,4,2,128]{1,3,4,2,0:T(2,128)(2,1)S(1)}, bf16[1,64,4,2,128]{1,3,4,2,0:T(2,128)(2,1)S(1)}, u32[]{:S(2)}, u32[]{:S(2)}) collective-permute-start(bf16[1,64,4,2,128]{1,3,4,2,0:T(2,128)(2,1)S(1)} %slice_bitcast_fusion.29), channel_id=1, source_target_pairs={{0,4},{4,8},{8,12},{1,5},{5,9},{9,13},{2,6},{6,10},{10,14},{3,7},{... | collective-permute-start | bytes 393224 | tf_op jit(solution)/shard_map/ppermute | solution.py:79
  124.0 10.4 %collective-permute-start.3 = (bf16[1,64,4,2,128]{1,3,4,2,0:T(2,128)(2,1)}, bf16[1,64,4,2,128]{1,3,4,2,0:T(2,128)(2,1)}, u32[]{:S(2)}, u32[]{:S(2)}) collective-permute-start(bf16[1,64,4,2,128]{1,3,4,2,0:T(2,128)(2,1)} %slice_bitcast_fusion.28), channel_id=1, source_target_pairs={{0,4},{4,8},{8,12},{1,5},{5,9},{9,13},{2,6},{6,10},{10,14},{3,7},{... | collective-permute-start | bytes 393224 | tf_op jit(solution)/shard_map/ppermute | solution.py:79
  160.2 10.8 %collective-permute-start.4 = (bf16[1,64,4,2,128]{1,3,4,2,0:T(2,128)(2,1)}, bf16[1,64,4,2,128]{1,3,4,2,0:T(2,128)(2,1)}, u32[]{:S(2)}, u32[]{:S(2)}) collective-permute-start(bf16[1,64,4,2,128]{1,3,4,2,0:T(2,128)(2,1)} %slice_bitcast_fusion.27), channel_id=1, source_target_pairs={{0,4},{4,8},{8,12},{1,5},{5,9},{9,13},{2,6},{6,10},{10,14},{3,7},{... | collective-permute-start | bytes 393224 | tf_op jit(solution)/shard_map/ppermute | solution.py:79
  199.8 10.0 %collective-permute-start.5 = (bf16[1,64,4,2,128]{1,3,4,2,0:T(2,128)(2,1)}, bf16[1,64,4,2,128]{1,3,4,2,0:T(2,128)(2,1)}, u32[]{:S(2)}, u32[]{:S(2)}) collective-permute-start(bf16[1,64,4,2,128]{1,3,4,2,0:T(2,128)(2,1)} %slice_bitcast_fusion.26), channel_id=1, source_target_pairs={{0,4},{4,8},{8,12},{1,5},{5,9},{9,13},{2,6},{6,10},{10,14},{3,7},{... | collective-permute-start | bytes 393224 | tf_op jit(solution)/shard_map/ppermute | solution.py:79
  238.1 10.3 %collective-permute-start.6 = (bf16[1,64,4,2,128]{1,3,4,2,0:T(2,128)(2,1)}, bf16[1,64,4,2,128]{1,3,4,2,0:T(2,128)(2,1)}, u32[]{:S(2)}, u32[]{:S(2)}) collective-permute-start(bf16[1,64,4,2,128]{1,3,4,2,0:T(2,128)(2,1)} %slice_bitcast_fusion.25), channel_id=1, source_target_pairs={{0,4},{4,8},{8,12},{1,5},{5,9},{9,13},{2,6},{6,10},{10,14},{3,7},{... | collective-permute-start | bytes 393224 | tf_op jit(solution)/shard_map/ppermute | solution.py:79
  276.3 9.9 %collective-permute-start.7 = (bf16[1,64,4,2,128]{1,3,4,2,0:T(2,128)(2,1)S(1)}, bf16[1,64,4,2,128]{1,3,4,2,0:T(2,128)(2,1)S(1)}, u32[]{:S(2)}, u32[]{:S(2)}) collective-permute-start(bf16[1,64,4,2,128]{1,3,4,2,0:T(2,128)(2,1)S(1)} %slice_bitcast_fusion.24), channel_id=1, source_target_pairs={{0,4},{4,8},{8,12},{1,5},{5,9},{9,13},{2,6},{6,10},{10,14},{3,7},{... | collective-permute-start | bytes 393224 | tf_op jit(solution)/shard_map/ppermute | solution.py:79
  313.5 10.8 %collective-permute-start.8 = (bf16[1,64,4,2,128]{1,3,4,2,0:T(2,128)(2,1)}, bf16[1,64,4,2,128]{1,3,4,2,0:T(2,128)(2,1)}, u32[]{:S(2)}, u32[]{:S(2)}) collective-permute-start(bf16[1,64,4,2,128]{1,3,4,2,0:T(2,128)(2,1)} %slice_bitcast_fusion.23), channel_id=1, source_target_pairs={{0,4},{4,8},{8,12},{1,5},{5,9},{9,13},{2,6},{6,10},{10,14},{3,7},{... | collective-permute-start | bytes 393224 | tf_op jit(solution)/shard_map/ppermute | solution.py:79
  352.3 10.4 %collective-permute-start.9 = (bf16[1,64,4,2,128]{1,3,4,2,0:T(2,128)(2,1)}, bf16[1,64,4,2,128]{1,3,4,2,0:T(2,128)(2,1)}, u32[]{:S(2)}, u32[]{:S(2)}) collective-permute-start(bf16[1,64,4,2,128]{1,3,4,2,0:T(2,128)(2,1)} %slice_bitcast_fusion.22), channel_id=1, source_target_pairs={{0,4},{4,8},{8,12},{1,5},{5,9},{9,13},{2,6},{6,10},{10,14},{3,7},{... | collective-permute-start | bytes 393224 | tf_op jit(solution)/shard_map/ppermute | solution.py:79
  401.5 65.5 %reduce-scatter.14.cloned.1.call-start = ((), (), s32[]{:S(2)}) async-start(), calls=%async_computation.12 | async-start | bytes 655360 | tf_op jit(solution)/shard_map/reduce_scatter | solution.py:100
  427.7 9.6 %collective-permute-start.10 = (bf16[1,64,4,2,128]{1,3,4,2,0:T(2,128)(2,1)}, bf16[1,64,4,2,128]{1,3,4,2,0:T(2,128)(2,1)}, u32[]{:S(2)}, u32[]{:S(2)}) collective-permute-start(bf16[1,64,4,2,128]{1,3,4,2,0:T(2,128)(2,1)} %copy.486), channel_id=1, source_target_pairs={{4,0},{8,4},{12,8},{5,1},{9,5},{13,9},{6,2},{10,6},{14,10},{7,3},{... | collective-permute-start | bytes 393224 | tf_op jit(solution)/shard_map/ppermute | solution.py:104
  449.7 58.2 %reduce-scatter.16.cloned.1.call-start = ((), (), s32[]{:S(2)}) async-start(), calls=%async_computation.13 | async-start | bytes 655360 | tf_op jit(solution)/shard_map/reduce_scatter | solution.py:100
  468.7 9.5 %collective-permute-start.11 = (bf16[1,64,4,2,128]{1,3,4,2,0:T(2,128)(2,1)}, bf16[1,64,4,2,128]{1,3,4,2,0:T(2,128)(2,1)}, u32[]{:S(2)}, u32[]{:S(2)}) collective-permute-start(bf16[1,64,4,2,128]{1,3,4,2,0:T(2,128)(2,1)} %copy.497), channel_id=1, source_target_pairs={{4,0},{8,4},{12,8},{5,1},{9,5},{13,9},{6,2},{10,6},{14,10},{7,3},{... | collective-permute-start | bytes 393224 | tf_op jit(solution)/shard_map/ppermute | solution.py:104
  490.7 58.3 %reduce-scatter.18.cloned.1.call-start = ((), (), s32[]{:S(2)}) async-start(), calls=%async_computation.14 | async-start | bytes 655360 | tf_op jit(solution)/shard_map/reduce_scatter | solution.py:100
  509.7 9.5 %collective-permute-start.12 = (bf16[1,64,4,2,128]{1,3,4,2,0:T(2,128)(2,1)}, bf16[1,64,4,2,128]{1,3,4,2,0:T(2,128)(2,1)}, u32[]{:S(2)}, u32[]{:S(2)}) collective-permute-start(bf16[1,64,4,2,128]{1,3,4,2,0:T(2,128)(2,1)} %copy.508), channel_id=1, source_target_pairs={{4,0},{8,4},{12,8},{5,1},{9,5},{13,9},{6,2},{10,6},{14,10},{7,3},{... | collective-permute-start | bytes 393224 | tf_op jit(solution)/shard_map/ppermute | solution.py:104
  531.7 57.9 %reduce-scatter.20.cloned.1.call-start = ((), (), s32[]{:S(2)}) async-start(), calls=%async_computation.15 | async-start | bytes 655360 | tf_op jit(solution)/shard_map/reduce_scatter | solution.py:100
  550.8 9.6 %collective-permute-start.13 = (bf16[1,64,4,2,128]{1,3,4,2,0:T(2,128)(2,1)}, bf16[1,64,4,2,128]{1,3,4,2,0:T(2,128)(2,1)}, u32[]{:S(2)}, u32[]{:S(2)}) collective-permute-start(bf16[1,64,4,2,128]{1,3,4,2,0:T(2,128)(2,1)} %copy.519), channel_id=1, source_target_pairs={{4,0},{8,4},{12,8},{5,1},{9,5},{13,9},{6,2},{10,6},{14,10},{7,3},{... | collective-permute-start | bytes 393224 | tf_op jit(solution)/shard_map/ppermute | solution.py:104
  572.3 76.2 %reduce-scatter.22.cloned.1.call-start = ((), (), s32[]{:S(2)}) async-start(), calls=%async_computation.16 | async-start | bytes 655360 | tf_op jit(solution)/shard_map/reduce_scatter | solution.py:100
  591.3 9.5 %collective-permute-start.14 = (bf16[1,64,4,2,128]{1,3,4,2,0:T(2,128)(2,1)}, bf16[1,64,4,2,128]{1,3,4,2,0:T(2,128)(2,1)}, u32[]{:S(2)}, u32[]{:S(2)}) collective-permute-start(bf16[1,64,4,2,128]{1,3,4,2,0:T(2,128)(2,1)} %copy.530), channel_id=1, source_target_pairs={{4,0},{8,4},{12,8},{5,1},{9,5},{13,9},{6,2},{10,6},{14,10},{7,3},{... | collective-permute-start | bytes 393224 | tf_op jit(solution)/shard_map/ppermute | solution.py:104
  612.8 80.7 %reduce-scatter.24.cloned.1.call-start = ((), (), s32[]{:S(2)}) async-start(), calls=%async_computation.17 | async-start | bytes 655360 | tf_op jit(solution)/shard_map/reduce_scatter | solution.py:100
  649.6 20.3 %collective-permute-start.15 = (bf16[1,64,4,2,128]{1,3,4,2,0:T(2,128)(2,1)S(1)}, bf16[1,64,4,2,128]{1,3,4,2,0:T(2,128)(2,1)S(1)}, u32[]{:S(2)}, u32[]{:S(2)}) collective-permute-start(bf16[1,64,4,2,128]{1,3,4,2,0:T(2,128)(2,1)S(1)} %copy.541), channel_id=1, source_target_pairs={{4,0},{8,4},{12,8},{5,1},{9,5},{13,9},{6,2},{10,6},{14,10},{7,3},{... | collective-permute-start | bytes 393224 | tf_op jit(solution)/shard_map/ppermute | solution.py:104
  674.9 63.8 %reduce-scatter.26.cloned.1.call-start = ((), (), s32[]{:S(2)}) async-start(), calls=%async_computation.18 | async-start | bytes 655360 | tf_op jit(solution)/shard_map/reduce_scatter | solution.py:100
  694.6 20.9 %collective-permute-start.16 = (bf16[1,64,4,2,128]{1,3,4,2,0:T(2,128)(2,1)S(1)}, bf16[1,64,4,2,128]{1,3,4,2,0:T(2,128)(2,1)S(1)}, u32[]{:S(2)}, u32[]{:S(2)}) collective-permute-start(bf16[1,64,4,2,128]{1,3,4,2,0:T(2,128)(2,1)S(1)} %copy.552), channel_id=1, source_target_pairs={{4,0},{8,4},{12,8},{5,1},{9,5},{13,9},{6,2},{10,6},{14,10},{7,3},{... | collective-permute-start | bytes 393224 | tf_op jit(solution)/shard_map/ppermute | solution.py:104
  720.5 62.7 %reduce-scatter.28.cloned.1.call-start = ((), (), s32[]{:S(2)}) async-start(), calls=%async_computation.19 | async-start | bytes 655360 | tf_op jit(solution)/shard_map/reduce_scatter | solution.py:100
  739.7 21.0 %collective-permute-start.17 = (bf16[1,64,4,2,128]{1,3,4,2,0:T(2,128)(2,1)S(1)}, bf16[1,64,4,2,128]{1,3,4,2,0:T(2,128)(2,1)S(1)}, u32[]{:S(2)}, u32[]{:S(2)}) collective-permute-start(bf16[1,64,4,2,128]{1,3,4,2,0:T(2,128)(2,1)S(1)} %copy.562), channel_id=1, source_target_pairs={{4,0},{8,4},{12,8},{5,1},{9,5},{13,9},{6,2},{10,6},{14,10},{7,3},{... | collective-permute-start | bytes 393224 | tf_op jit(solution)/shard_map/ppermute | solution.py:104
  765.1 62.7 %reduce-scatter.30.cloned.1.call-start = ((), (), s32[]{:S(2)}) async-start(), calls=%async_computation.20 | async-start | bytes 655360 | tf_op jit(solution)/shard_map/reduce_scatter | solution.py:100
  784.2 21.0 %collective-permute-start.18 = (bf16[1,64,4,2,128]{1,3,4,2,0:T(2,128)(2,1)S(1)}, bf16[1,64,4,2,128]{1,3,4,2,0:T(2,128)(2,1)S(1)}, u32[]{:S(2)}, u32[]{:S(2)}) collective-permute-start(bf16[1,64,4,2,128]{1,3,4,2,0:T(2,128)(2,1)S(1)} %copy.572), channel_id=1, source_target_pairs={{4,0},{8,4},{12,8},{5,1},{9,5},{13,9},{6,2},{10,6},{14,10},{7,3},{... | collective-permute-start | bytes 393224 | tf_op jit(solution)/shard_map/ppermute | solution.py:104
  809.7 86.4 %reduce-scatter.32.cloned.1.call-start = ((), (), s32[]{:S(2)}) async-start(), calls=%async_computation.21 | async-start | bytes 655360 | tf_op jit(solution)/shard_map/reduce_scatter | solution.py:100
  828.8 20.9 %collective-permute-start.19 = (bf16[1,64,4,2,128]{1,3,4,2,0:T(2,128)(2,1)S(1)}, bf16[1,64,4,2,128]{1,3,4,2,0:T(2,128)(2,1)S(1)}, u32[]{:S(2)}, u32[]{:S(2)}) collective-permute-start(bf16[1,64,4,2,128]{1,3,4,2,0:T(2,128)(2,1)S(1)} %copy.582), channel_id=1, source_target_pairs={{4,0},{8,4},{12,8},{5,1},{9,5},{13,9},{6,2},{10,6},{14,10},{7,3},{... | collective-permute-start | bytes 393224 | tf_op jit(solution)/shard_map/ppermute | solution.py:104
  870.9 26.1 %copy-start.54 = (bf16[64,8,128]{2,0,1:T(8,128)(2,1)S(1)}, bf16[64,8,128]{2,0,1:T(8,128)(2,1)}, u32[]{:S(2)}) copy-start(bf16[64,8,128]{2,0,1:T(8,128)(2,1)} %reduce-scatter.24.cloned.1.call-done) | copy-start | bytes 393220
  (63 other events, 620.5 us)
Sparse Core Ops, SparseCore 0:
  401.6 24.2 reduce-scatter.11
  449.8 17.0 reduce-scatter.13
  490.8 17.0 reduce-scatter.15
  531.8 17.1 reduce-scatter.17
  572.4 17.1 reduce-scatter.19
  612.9 17.0 reduce-scatter.21
  675.0 18.4 reduce-scatter.23
  720.6 17.9 reduce-scatter.25
  765.2 17.9 reduce-scatter.27
  809.8 17.8 reduce-scatter.29
  854.2 17.8 reduce-scatter.31
where the time goes:
time: 918 us; the launch traced here: 907 us
  matrix products  261 us (28%)
  local copies, waits for them, and re-layouts  210 us (23%)
  blocking collectives  150 us (16%)
  waiting for transfers between devices  131 us (14%)
  starting transfers between devices  109 us (12%)
  other arithmetic  29.2 us (3%)
  between operations  16 us (2%)
    conv_general_dilated x11, matrix products, conv_weight_grad(): lax.conv_general_dilated(act, slope, (1, 1, 1), PAD3, dimension_numbers=(...  195 us
    all_gather x11, blocking collectives, local(): full_input = lax.all_gather(own_input, 'filt', axis=1, tiled=True)  150 us
    reduce_scatter x11, waiting for transfers between devices, local(): lax.psum_scatter(partial, 'filt', scatter_dimension=0, tiled=True)  96.3 us
    ppermute x10, starting transfers between devices, local(): incoming = lax.ppermute(outgoing, 'section', forward_pairs)  66.7 us
    unnamed x176, local copies, waits for them, and re-layouts  58.6 us
    conv_general_dilated x11, matrix products, conv_forward(): lax.conv_general_dilated(act, kernel, (1, 1, 1), PAD3, dimension_numbers=...  52.9 us
    all_gather x33, local copies, waits for them, and re-layouts, local(): full_input = lax.all_gather(own_input, 'filt', axis=1, tiled=True)  43 us
    ppermute x10, starting transfers between devices, local(): incoming = lax.ppermute(input_grad, 'section', backward_pairs)  41.7 us
  transfers between devices with their start and end apart: 31, of which 22 were waited for; matrix products, arithmetic and copies ran while one was open for 28% of the time, Pallas kernels for 0%

commit v1 on v0

--- a/solution.py
+++ b/solution.py
@@ -6,6 +6,24 @@
 
 CHUNK = 1
 PAD3 = ((1, 1), (1, 1), (1, 1))
+
+
+def collect(shard, axis, dim):
+    ways, here, turn = (lax.axis_size(axis), lax.axis_index(axis), shard.shape[dim])
+    dims = [n * ways if d == dim else n for d, n in enumerate(shard.shape)]
+    full = lax.dynamic_update_slice_in_dim(
+        jnp.zeros(dims, shard.dtype), shard, here * turn, axis=dim
+    )
+    going_up = going_down = shard
+    for far in range(1, ways // 2 + 1):
+        going_up = lax.ppermute(going_up, axis, [(d, (d + 1) % ways) for d in range(ways)])
+        full = lax.dynamic_update_slice_in_dim(full, going_up, (here - far) % ways * turn, axis=dim)
+        if 2 * far < ways:
+            going_down = lax.ppermute(going_down, axis, [(d, (d - 1) % ways) for d in range(ways)])
+            full = lax.dynamic_update_slice_in_dim(
+                full, going_down, (here + far) % ways * turn, axis=dim
+            )
+    return full
 
 
 def silu_slope(pre_act):
@@ -70,7 +88,7 @@
         else:
             first = jnp.zeros(slab, jnp.bfloat16)
         own_input = jnp.where(section_pos == 0, first, incoming)
-        full_input = lax.all_gather(own_input, "filt", axis=1, tiled=True)
+        full_input = collect(own_input, "filt", 1)
         pre_act = conv_forward(full_input, kernel) + layer_bias
         gathered.append(full_input)
         pres.append(pre_act)

time: 918 us -> 770 us (0.84)
  blocking collectives: 150 us -> 0 us
  local copies, waits for them, and re-layouts: 210 us -> 126 us
  waiting for transfers between devices: 131 us -> 192 us
  starting transfers between devices: 109 us -> 146 us
  other arithmetic: 29.2 us -> 15.7 us
    all_gather x11 -> x0, blocking collectives: 150 us -> none  [local(): full_input = lax.all_gather(own_input, 'filt', axis=1, tiled=True)]
    ppermute x0 -> x33, waiting for transfers between devices: none -> 76.6 us  [the longest x22 74.2 us: collect(): lax.ppermute(going_up, axis, [(d, (d + 1) % ways) for d in range(ways)])]
    all_gather x33 -> x0, local copies, waits for them, and re-layouts: 43 us -> none  [local(): full_input = lax.all_gather(own_input, 'filt', axis=1, tiled=True)]
    dynamic_update_slice x0 -> x55, local copies, waits for them, and re-layouts: none -> 41.1 us  [the longest x44 36.2 us: collect(): lax.dynamic_update_slice_in_dim(full, going_up, (here - far) % ways * tur...]
    ppermute x0 -> x33, starting transfers between devices: none -> 38.5 us  [the longest x11 34.7 us: collect(): lax.ppermute(going_down, axis, [(d, (d - 1) % ways) for d in range(ways)])]
    unnamed x176 -> x169, local copies, waits for them, and re-layouts: 58.6 us -> 27.6 us
    select_n x11 -> x0, local copies, waits for them, and re-layouts: 12.4 us -> none  [local(): own_input = jnp.where(section_pos == 0, first, incoming)]
    select_n x11 -> x0, other arithmetic: 11 us -> none  [local(): own_input = jnp.where(section_pos == 0, first, incoming)]
  transfers between devices with their start and end apart: 31 -> 64, of which waited for: 22 -> 41; matrix products, arithmetic and copies ran while one was open for 28% -> 34% of each run, Pallas kernels for 0% -> 0%
where the time goes in v1:
time: 770 us; the launch traced here: 760 us
  matrix products  264 us (34%)
  waiting for transfers between devices  192 us (25%)
  starting transfers between devices  146 us (19%)
  local copies, waits for them, and re-layouts  126 us (16%)
  between operations  16.7 us (2%)
  other arithmetic  15.7 us (2%)
    conv_general_dilated x11, matrix products, conv_weight_grad(): lax.conv_general_dilated(act, slope, (1, 1, 1), PAD3, dimension_numbers=(...  198 us
    reduce_scatter x11, waiting for transfers between devices, local(): lax.psum_scatter(partial, 'filt', scatter_dimension=0, tiled=True)  89.8 us
    ppermute x22, waiting for transfers between devices, collect(): lax.ppermute(going_up, axis, [(d, (d + 1) % ways) for d in range(ways)])  74.2 us
    ppermute x10, starting transfers between devices, local(): incoming = lax.ppermute(outgoing, 'section', forward_pairs)  65.8 us
    conv_general_dilated x11, matrix products, conv_forward(): lax.conv_general_dilated(act, kernel, (1, 1, 1), PAD3, dimension_numbers=...  52.9 us
    ppermute x10, starting transfers between devices, local(): incoming = lax.ppermute(input_grad, 'section', backward_pairs)  40.8 us
    dynamic_update_slice x44, local copies, waits for them, and re-layouts, collect(): lax.dynamic_update_slice_in_dim(full, going_up, (here - far) % ways * tur...  36.2 us
    ppermute x11, starting transfers between devices, collect(): lax.ppermute(going_down, axis, [(d, (d - 1) % ways) for d in range(ways)])  34.7 us
  transfers between devices with their start and end apart: 64, of which 41 were waited for; matrix products, arithmetic and copies ran while one was open for 34% of the time, Pallas kernels for 0%

profile of v1, /device:TPU:1, one launch (start us, length us, event | category | flops | bytes accessed | tf_op | source)
XLA Modules:
  0.0 760.4 jit_solution(13712565885226044805)
XLA Ops:
  29.1 6.5 collective-permute-start.3
  58.8 6.1 collective-permute-start.7
  88.2 6.7 collective-permute-start.11
  112.2 4.9 multiply_convert_fusion.6
  117.6 6.7 collective-permute-start.15
  147.1 6.7 collective-permute-start.19
  176.6 6.7 collective-permute-start.23
  206.2 6.6 collective-permute-start.27
  230.1 4.9 multiply_convert_fusion.2
  235.6 6.7 collective-permute-start.31
  250.4 5.5 collective-permute-done.34
  262.4 6.7 collective-permute-start.35
  276.9 5.5 collective-permute-done.38
  283.5 4.9 multiply_convert_fusion
  288.9 6.7 collective-permute-start.39
  304.2 5.5 collective-permute-done.42
  321.4 20.9 %reduce-scatter.12.cloned.1.call-done = bf16[64,8,128]{2,0,1:T(8,128)(2,1)} async-done(((bf16[256,8,128]{2,0,1:T(8,128)(2,1)}), bf16[64,8,128]{2,0,1:T(8,128)(2,1)}) %reduce-scatter.12.cloned.1.call-update) | async-done | bytes 131088 | tf_op jit(solution)/shard_map/reduce_scatter | solution.py:118
  355.9 17.2 %reduce-scatter.14.cloned.1.call-done = bf16[64,8,128]{2,0,1:T(8,128)(2,1)} async-done(((bf16[256,8,128]{2,0,1:T(8,128)(2,1)}), bf16[64,8,128]{2,0,1:T(8,128)(2,1)}) %reduce-scatter.14.cloned.1.call-update) | async-done | bytes 131088 | tf_op jit(solution)/shard_map/reduce_scatter | solution.py:118
  386.9 17.2 %reduce-scatter.16.cloned.1.call-done = bf16[64,8,128]{2,0,1:T(8,128)(2,1)} async-done(((bf16[256,8,128]{2,0,1:T(8,128)(2,1)}), bf16[64,8,128]{2,0,1:T(8,128)(2,1)}) %reduce-scatter.16.cloned.1.call-update) | async-done | bytes 131088 | tf_op jit(solution)/shard_map/reduce_scatter | solution.py:118
  417.6 17.3 %reduce-scatter.18.cloned.1.call-done = bf16[64,8,128]{2,0,1:T(8,128)(2,1)} async-done(((bf16[256,8,128]{2,0,1:T(8,128)(2,1)}), bf16[64,8,128]{2,0,1:T(8,128)(2,1)}) %reduce-scatter.18.cloned.1.call-update) | async-done | bytes 131088 | tf_op jit(solution)/shard_map/reduce_scatter | solution.py:118
  448.0 17.1 %reduce-scatter.20.cloned.1.call-done = bf16[64,8,128]{2,0,1:T(8,128)(2,1)} async-done(((bf16[256,8,128]{2,0,1:T(8,128)(2,1)}), bf16[64,8,128]{2,0,1:T(8,128)(2,1)}) %reduce-scatter.20.cloned.1.call-update) | async-done | bytes 131088 | tf_op jit(solution)/shard_map/reduce_scatter | solution.py:118
  507.1 18.0 %fusion.301 = f32[64,3,3,3,256]{4,0,3,2,1:T(8,128)} fusion(bf16[1,256,4,2,128]{1,0,4,3,2:T(2,128)(2,1)S(1)} %copy-done.32, bf16[1,64,4,2,128]{1,0,4,3,2:T(2,128)(2,1)} %copy.294), kind=kOutput, calls=%fused_computation.432 | convolution fusion | flops 500695040 | bytes 2424832 | tf_op jit(solution)/shard_map/conv_general_dilated | solution.py:58
  529.0 16.6 %fusion.302 = f32[64,3,3,3,256]{4,0,3,2,1:T(8,128)} fusion(bf16[1,256,4,2,128]{1,0,4,3,2:T(2,128)(2,1)S(1)} %copy-done.31, bf16[1,64,4,2,128]{1,0,4,3,2:T(2,128)(2,1)S(1)} %copy.304), kind=kOutput, calls=%fused_computation.433 | convolution fusion | flops 500695040 | bytes 2424832 | tf_op jit(solution)/shard_map/conv_general_dilated | solution.py:58
  550.0 18.2 %fusion.303 = f32[64,3,3,3,256]{4,0,3,2,1:T(8,128)} fusion(bf16[1,256,4,2,128]{1,0,4,3,2:T(2,128)(2,1)} %copy.313, bf16[1,64,4,2,128]{1,0,4,3,2:T(2,128)(2,1)S(1)} %copy.314), kind=kOutput, calls=%fused_computation.434 | convolution fusion | flops 500695040 | bytes 2424832 | tf_op jit(solution)/shard_map/conv_general_dilated | solution.py:58
  572.4 16.7 %fusion.304 = f32[64,3,3,3,256]{4,0,3,2,1:T(8,128)} fusion(bf16[1,256,4,2,128]{1,0,4,3,2:T(2,128)(2,1)S(1)} %copy-done.30, bf16[1,64,4,2,128]{1,0,4,3,2:T(2,128)(2,1)S(1)} %copy.324), kind=kOutput, calls=%fused_computation.435 | convolution fusion | flops 500695040 | bytes 2424832 | tf_op jit(solution)/shard_map/conv_general_dilated | solution.py:58
  593.4 18.2 %fusion.305 = f32[64,3,3,3,256]{4,0,3,2,1:T(8,128)} fusion(bf16[1,256,4,2,128]{1,0,4,3,2:T(2,128)(2,1)} %copy.333, bf16[1,64,4,2,128]{1,0,4,3,2:T(2,128)(2,1)S(1)} %copy.334), kind=kOutput, calls=%fused_computation.436 | convolution fusion | flops 500695040 | bytes 2424832 | tf_op jit(solution)/shard_map/conv_general_dilated | solution.py:58
  615.7 16.6 %fusion.306 = f32[64,3,3,3,256]{4,0,3,2,1:T(8,128)} fusion(bf16[1,256,4,2,128]{1,0,4,3,2:T(2,128)(2,1)S(1)} %copy-done.29, bf16[1,64,4,2,128]{1,0,4,3,2:T(2,128)(2,1)S(1)} %copy.344), kind=kOutput, calls=%fused_computation.437 | convolution fusion | flops 500695040 | bytes 2424832 | tf_op jit(solution)/shard_map/conv_general_dilated | solution.py:58
  637.3 18.0 %fusion.307 = f32[64,3,3,3,256]{4,0,3,2,1:T(8,128)} fusion(bf16[1,256,4,2,128]{1,0,4,3,2:T(2,128)(2,1)S(1)} %copy-done.28, bf16[1,64,4,2,128]{1,0,4,3,2:T(2,128)(2,1)} %copy.354), kind=kOutput, calls=%fused_computation.438 | convolution fusion | flops 500695040 | bytes 2424832 | tf_op jit(solution)/shard_map/conv_general_dilated | solution.py:58
  659.6 16.6 %fusion.308 = f32[64,3,3,3,256]{4,0,3,2,1:T(8,128)} fusion(bf16[1,256,4,2,128]{1,0,4,3,2:T(2,128)(2,1)S(1)} %copy-done.27, bf16[1,64,4,2,128]{1,0,4,3,2:T(2,128)(2,1)S(1)} %copy.364), kind=kOutput, calls=%fused_computation.439 | convolution fusion | flops 500695040 | bytes 2424832 | tf_op jit(solution)/shard_map/conv_general_dilated | solution.py:58
  681.2 17.9 %fusion.309 = f32[64,3,3,3,256]{4,0,3,2,1:T(8,128)} fusion(bf16[1,256,4,2,128]{1,0,4,3,2:T(2,128)(2,1)S(1)} %copy-done.26, bf16[1,64,4,2,128]{1,0,4,3,2:T(2,128)(2,1)} %copy.373), kind=kOutput, calls=%fused_computation.440 | convolution fusion | flops 500695040 | bytes 2424832 | tf_op jit(solution)/shard_map/conv_general_dilated | solution.py:58
  703.7 16.6 %fusion.310 = f32[64,3,3,3,256]{4,0,3,2,1:T(8,128)} fusion(bf16[1,256,4,2,128]{1,0,4,3,2:T(2,128)(2,1)S(1)} %copy-done.25, bf16[1,64,4,2,128]{1,0,4,3,2:T(2,128)(2,1)S(1)} %copy.382), kind=kOutput, calls=%fused_computation.441 | convolution fusion | flops 500695040 | bytes 2424832 | tf_op jit(solution)/shard_map/conv_general_dilated | solution.py:58
  724.6 24.3 %add_multiply_fusion = f32[64,3,3,3,256]{4,0,3,2,1:T(8,128)} fusion(f32[64,3,3,3,256]{4,0,3,2,1:T(8,128)} %fusion.310, f32[64,3,3,3,256]{4,0,3,2,1:T(8,128)} %fusion.309, f32[64,3,3,3,256]{4,0,3,2,1:T(8,128)} %fusion.308, f32[64,3,3,3,256]{4,0,3,2,1:T(8,128)} %fusion.307, f32[64,3,3,3,256]{4,0,3,2,1:T(8,128)} %fusion.306, f32[64,3,3,3,256]{4,0,3,2,1:T(8,128)} %fusion.305, ...), kind=kOutput, calls=%fused_computation | convolution fusion | flops 505561088 | bytes 20119552 | tf_op jit(solution)/shard_map/conv_general_dilated | solution.py:58
  (544 shorter events, 359.1 us)
Async XLA Ops:
  7.2 335.1 %reduce-scatter.12.cloned.1.call-start = ((), (), s32[]{:S(2)}) async-start(), calls=%async_computation.11 | async-start | bytes 655360 | tf_op jit(solution)/shard_map/reduce_scatter | solution.py:118
  11.6 7.7 %collective-permute-start.1 = (bf16[1,64,4,2,128]{4,1,3,2,0:T(8,128)(2,1)S(1)}, bf16[1,64,4,2,128]{4,1,3,2,0:T(8,128)(2,1)S(1)}, u32[]{:S(2)}, u32[]{:S(2)}) collective-permute-start(bf16[1,64,4,2,128]{4,1,3,2,0:T(8,128)(2,1)S(1)} %get-tuple-element.46), channel_id=1, source_target_pairs={{0,3},{1,0},{2,1},{3,2},{4,7},{5,4},{6,5},{7,6},{8,11},{9,8},{10,9... | collective-permute-start | bytes 393224 | tf_op jit(solution)/shard_map/ppermute | solution.py:22
  29.1 8.4 %collective-permute-start.3 = (bf16[1,64,4,2,128]{4,1,3,2,0:T(8,128)(2,1)S(1)}, bf16[1,64,4,2,128]{4,1,3,2,0:T(8,128)(2,1)S(1)}, u32[]{:S(2)}, u32[]{:S(2)}) collective-permute-start(bf16[1,64,4,2,128]{4,1,3,2,0:T(8,128)(2,1)S(1)} %bitcast.467), channel_id=1, source_target_pairs={{0,4},{4,8},{8,12},{1,5},{5,9},{9,13},{2,6},{6,10},{10,14},{3,7},{... | collective-permute-start | bytes 393224 | tf_op jit(solution)/shard_map/ppermute | solution.py:97
  58.8 8.1 %collective-permute-start.7 = (bf16[1,64,4,2,128]{4,1,3,2,0:T(8,128)(2,1)S(1)}, bf16[1,64,4,2,128]{4,1,3,2,0:T(8,128)(2,1)S(1)}, u32[]{:S(2)}, u32[]{:S(2)}) collective-permute-start(bf16[1,64,4,2,128]{4,1,3,2,0:T(8,128)(2,1)S(1)} %bitcast.468), channel_id=1, source_target_pairs={{0,4},{4,8},{8,12},{1,5},{5,9},{9,13},{2,6},{6,10},{10,14},{3,7},{... | collective-permute-start | bytes 393224 | tf_op jit(solution)/shard_map/ppermute | solution.py:97
  88.2 8.6 %collective-permute-start.11 = (bf16[1,64,4,2,128]{4,1,3,2,0:T(8,128)(2,1)S(1)}, bf16[1,64,4,2,128]{4,1,3,2,0:T(8,128)(2,1)S(1)}, u32[]{:S(2)}, u32[]{:S(2)}) collective-permute-start(bf16[1,64,4,2,128]{4,1,3,2,0:T(8,128)(2,1)S(1)} %bitcast.469), channel_id=1, source_target_pairs={{0,4},{4,8},{8,12},{1,5},{5,9},{9,13},{2,6},{6,10},{10,14},{3,7},{... | collective-permute-start | bytes 393224 | tf_op jit(solution)/shard_map/ppermute | solution.py:97
  117.6 8.6 %collective-permute-start.15 = (bf16[1,64,4,2,128]{4,1,3,2,0:T(8,128)(2,1)S(1)}, bf16[1,64,4,2,128]{4,1,3,2,0:T(8,128)(2,1)S(1)}, u32[]{:S(2)}, u32[]{:S(2)}) collective-permute-start(bf16[1,64,4,2,128]{4,1,3,2,0:T(8,128)(2,1)S(1)} %bitcast.470), channel_id=1, source_target_pairs={{0,4},{4,8},{8,12},{1,5},{5,9},{9,13},{2,6},{6,10},{10,14},{3,7},{... | collective-permute-start | bytes 393224 | tf_op jit(solution)/shard_map/ppermute | solution.py:97
  147.1 8.6 %collective-permute-start.19 = (bf16[1,64,4,2,128]{4,1,3,2,0:T(8,128)(2,1)S(1)}, bf16[1,64,4,2,128]{4,1,3,2,0:T(8,128)(2,1)S(1)}, u32[]{:S(2)}, u32[]{:S(2)}) collective-permute-start(bf16[1,64,4,2,128]{4,1,3,2,0:T(8,128)(2,1)S(1)} %bitcast.471), channel_id=1, source_target_pairs={{0,4},{4,8},{8,12},{1,5},{5,9},{9,13},{2,6},{6,10},{10,14},{3,7},{... | collective-permute-start | bytes 393224 | tf_op jit(solution)/shard_map/ppermute | solution.py:97
  176.6 8.6 %collective-permute-start.23 = (bf16[1,64,4,2,128]{4,1,3,2,0:T(8,128)(2,1)S(1)}, bf16[1,64,4,2,128]{4,1,3,2,0:T(8,128)(2,1)S(1)}, u32[]{:S(2)}, u32[]{:S(2)}) collective-permute-start(bf16[1,64,4,2,128]{4,1,3,2,0:T(8,128)(2,1)S(1)} %bitcast.472), channel_id=1, source_target_pairs={{0,4},{4,8},{8,12},{1,5},{5,9},{9,13},{2,6},{6,10},{10,14},{3,7},{... | collective-permute-start | bytes 393224 | tf_op jit(solution)/shard_map/ppermute | solution.py:97
  206.2 8.6 %collective-permute-start.27 = (bf16[1,64,4,2,128]{4,1,3,2,0:T(8,128)(2,1)S(1)}, bf16[1,64,4,2,128]{4,1,3,2,0:T(8,128)(2,1)S(1)}, u32[]{:S(2)}, u32[]{:S(2)}) collective-permute-start(bf16[1,64,4,2,128]{4,1,3,2,0:T(8,128)(2,1)S(1)} %bitcast.473), channel_id=1, source_target_pairs={{0,4},{4,8},{8,12},{1,5},{5,9},{9,13},{2,6},{6,10},{10,14},{3,7},{... | collective-permute-start | bytes 393224 | tf_op jit(solution)/shard_map/ppermute | solution.py:97
  235.6 8.6 %collective-permute-start.31 = (bf16[1,64,4,2,128]{4,1,3,2,0:T(8,128)(2,1)S(1)}, bf16[1,64,4,2,128]{4,1,3,2,0:T(8,128)(2,1)S(1)}, u32[]{:S(2)}, u32[]{:S(2)}) collective-permute-start(bf16[1,64,4,2,128]{4,1,3,2,0:T(8,128)(2,1)S(1)} %bitcast.474), channel_id=1, source_target_pairs={{0,4},{4,8},{8,12},{1,5},{5,9},{9,13},{2,6},{6,10},{10,14},{3,7},{... | collective-permute-start | bytes 393224 | tf_op jit(solution)/shard_map/ppermute | solution.py:97
  262.4 8.6 %collective-permute-start.35 = (bf16[1,64,4,2,128]{4,1,3,2,0:T(8,128)(2,1)S(1)}, bf16[1,64,4,2,128]{4,1,3,2,0:T(8,128)(2,1)S(1)}, u32[]{:S(2)}, u32[]{:S(2)}) collective-permute-start(bf16[1,64,4,2,128]{4,1,3,2,0:T(8,128)(2,1)S(1)} %bitcast.475), channel_id=1, source_target_pairs={{0,4},{4,8},{8,12},{1,5},{5,9},{9,13},{2,6},{6,10},{10,14},{3,7},{... | collective-permute-start | bytes 393224 | tf_op jit(solution)/shard_map/ppermute | solution.py:97
  288.9 8.6 %collective-permute-start.39 = (bf16[1,64,4,2,128]{4,1,3,2,0:T(8,128)(2,1)S(1)}, bf16[1,64,4,2,128]{4,1,3,2,0:T(8,128)(2,1)S(1)}, u32[]{:S(2)}, u32[]{:S(2)}) collective-permute-start(bf16[1,64,4,2,128]{4,1,3,2,0:T(8,128)(2,1)S(1)} %bitcast.476), channel_id=1, source_target_pairs={{0,4},{4,8},{8,12},{1,5},{5,9},{9,13},{2,6},{6,10},{10,14},{3,7},{... | collective-permute-start | bytes 393224 | tf_op jit(solution)/shard_map/ppermute | solution.py:97
  321.4 51.8 %reduce-scatter.14.cloned.1.call-start = ((), (), s32[]{:S(2)}) async-start(), calls=%async_computation.12 | async-start | bytes 655360 | tf_op jit(solution)/shard_map/reduce_scatter | solution.py:118
  342.3 8.1 %collective-permute-start.43 = (bf16[1,64,4,2,128]{4,1,3,2,0:T(8,128)(2,1)}, bf16[1,64,4,2,128]{4,1,3,2,0:T(8,128)(2,1)}, u32[]{:S(2)}, u32[]{:S(2)}) collective-permute-start(bf16[1,64,4,2,128]{4,1,3,2,0:T(8,128)(2,1)} %bitcast.477), channel_id=1, source_target_pairs={{4,0},{8,4},{12,8},{5,1},{9,5},{13,9},{6,2},{10,6},{14,10},{7,3},{... | collective-permute-start | bytes 393224 | tf_op jit(solution)/shard_map/ppermute | solution.py:122
  355.9 48.2 %reduce-scatter.16.cloned.1.call-start = ((), (), s32[]{:S(2)}) async-start(), calls=%async_computation.13 | async-start | bytes 655360 | tf_op jit(solution)/shard_map/reduce_scatter | solution.py:118
  373.2 8.3 %collective-permute-start.44 = (bf16[1,64,4,2,128]{4,1,3,2,0:T(8,128)(2,1)}, bf16[1,64,4,2,128]{4,1,3,2,0:T(8,128)(2,1)}, u32[]{:S(2)}, u32[]{:S(2)}) collective-permute-start(bf16[1,64,4,2,128]{4,1,3,2,0:T(8,128)(2,1)} %bitcast.479), channel_id=1, source_target_pairs={{4,0},{8,4},{12,8},{5,1},{9,5},{13,9},{6,2},{10,6},{14,10},{7,3},{... | collective-permute-start | bytes 393224 | tf_op jit(solution)/shard_map/ppermute | solution.py:122
  386.8 48.1 %reduce-scatter.18.cloned.1.call-start = ((), (), s32[]{:S(2)}) async-start(), calls=%async_computation.14 | async-start | bytes 655360 | tf_op jit(solution)/shard_map/reduce_scatter | solution.py:118
  404.0 8.1 %collective-permute-start.45 = (bf16[1,64,4,2,128]{4,1,3,2,0:T(8,128)(2,1)}, bf16[1,64,4,2,128]{4,1,3,2,0:T(8,128)(2,1)}, u32[]{:S(2)}, u32[]{:S(2)}) collective-permute-start(bf16[1,64,4,2,128]{4,1,3,2,0:T(8,128)(2,1)} %bitcast.481), channel_id=1, source_target_pairs={{4,0},{8,4},{12,8},{5,1},{9,5},{13,9},{6,2},{10,6},{14,10},{7,3},{... | collective-permute-start | bytes 393224 | tf_op jit(solution)/shard_map/ppermute | solution.py:122
  417.6 47.6 %reduce-scatter.20.cloned.1.call-start = ((), (), s32[]{:S(2)}) async-start(), calls=%async_computation.15 | async-start | bytes 655360 | tf_op jit(solution)/shard_map/reduce_scatter | solution.py:118
  434.9 8.2 %collective-permute-start.46 = (bf16[1,64,4,2,128]{4,1,3,2,0:T(8,128)(2,1)}, bf16[1,64,4,2,128]{4,1,3,2,0:T(8,128)(2,1)}, u32[]{:S(2)}, u32[]{:S(2)}) collective-permute-start(bf16[1,64,4,2,128]{4,1,3,2,0:T(8,128)(2,1)} %bitcast.483), channel_id=1, source_target_pairs={{4,0},{8,4},{12,8},{5,1},{9,5},{13,9},{6,2},{10,6},{14,10},{7,3},{... | collective-permute-start | bytes 393224 | tf_op jit(solution)/shard_map/ppermute | solution.py:122
  448.0 77.4 %reduce-scatter.22.cloned.1.call-start = ((), (), s32[]{:S(2)}) async-start(), calls=%async_computation.16 | async-start | bytes 655360 | tf_op jit(solution)/shard_map/reduce_scatter | solution.py:118
  465.1 36.9 %collective-permute-start.47 = (bf16[1,64,4,2,128]{4,1,3,2,0:T(8,128)(2,1)}, bf16[1,64,4,2,128]{4,1,3,2,0:T(8,128)(2,1)}, u32[]{:S(2)}, u32[]{:S(2)}) collective-permute-start(bf16[1,64,4,2,128]{4,1,3,2,0:T(8,128)(2,1)} %bitcast.485), channel_id=1, source_target_pairs={{4,0},{8,4},{12,8},{5,1},{9,5},{13,9},{6,2},{10,6},{14,10},{7,3},{... | collective-permute-start | bytes 393224 | tf_op jit(solution)/shard_map/ppermute | solution.py:122
  506.8 61.7 %reduce-scatter.24.cloned.1.call-start = ((), (), s32[]{:S(2)}) async-start(), calls=%async_computation.17 | async-start | bytes 655360 | tf_op jit(solution)/shard_map/reduce_scatter | solution.py:118
  525.5 20.6 %collective-permute-start.48 = (bf16[1,64,4,2,128]{4,1,3,2,0:T(8,128)(2,1)}, bf16[1,64,4,2,128]{4,1,3,2,0:T(8,128)(2,1)S(1)}, u32[]{:S(2)}, u32[]{:S(2)}) collective-permute-start(bf16[1,64,4,2,128]{4,1,3,2,0:T(8,128)(2,1)} %bitcast.487), channel_id=1, source_target_pairs={{4,0},{8,4},{12,8},{5,1},{9,5},{13,9},{6,2},{10,6},{14,10},{7,3},{... | collective-permute-start | bytes 393224 | tf_op jit(solution)/shard_map/ppermute | solution.py:122
  549.9 62.0 %reduce-scatter.26.cloned.1.call-start = ((), (), s32[]{:S(2)}) async-start(), calls=%async_computation.18 | async-start | bytes 655360 | tf_op jit(solution)/shard_map/reduce_scatter | solution.py:118
  568.6 20.9 %collective-permute-start.49 = (bf16[1,64,4,2,128]{4,1,3,2,0:T(8,128)(2,1)}, bf16[1,64,4,2,128]{4,1,3,2,0:T(8,128)(2,1)S(1)}, u32[]{:S(2)}, u32[]{:S(2)}) collective-permute-start(bf16[1,64,4,2,128]{4,1,3,2,0:T(8,128)(2,1)} %bitcast.489), channel_id=1, source_target_pairs={{4,0},{8,4},{12,8},{5,1},{9,5},{13,9},{6,2},{10,6},{14,10},{7,3},{... | collective-permute-start | bytes 393224 | tf_op jit(solution)/shard_map/ppermute | solution.py:122
  593.3 62.3 %reduce-scatter.28.cloned.1.call-start = ((), (), s32[]{:S(2)}) async-start(), calls=%async_computation.19 | async-start | bytes 655360 | tf_op jit(solution)/shard_map/reduce_scatter | solution.py:118
  611.9 21.4 %collective-permute-start.50 = (bf16[1,64,4,2,128]{4,1,3,2,0:T(8,128)(2,1)}, bf16[1,64,4,2,128]{4,1,3,2,0:T(8,128)(2,1)S(1)}, u32[]{:S(2)}, u32[]{:S(2)}) collective-permute-start(bf16[1,64,4,2,128]{4,1,3,2,0:T(8,128)(2,1)} %bitcast.491), channel_id=1, source_target_pairs={{4,0},{8,4},{12,8},{5,1},{9,5},{13,9},{6,2},{10,6},{14,10},{7,3},{... | collective-permute-start | bytes 393224 | tf_op jit(solution)/shard_map/ppermute | solution.py:122
  637.2 62.3 %reduce-scatter.30.cloned.1.call-start = ((), (), s32[]{:S(2)}) async-start(), calls=%async_computation.20 | async-start | bytes 655360 | tf_op jit(solution)/shard_map/reduce_scatter | solution.py:118
  655.7 21.7 %collective-permute-start.51 = (bf16[1,64,4,2,128]{4,1,3,2,0:T(8,128)(2,1)}, bf16[1,64,4,2,128]{4,1,3,2,0:T(8,128)(2,1)S(1)}, u32[]{:S(2)}, u32[]{:S(2)}) collective-permute-start(bf16[1,64,4,2,128]{4,1,3,2,0:T(8,128)(2,1)} %bitcast.493), channel_id=1, source_target_pairs={{4,0},{8,4},{12,8},{5,1},{9,5},{13,9},{6,2},{10,6},{14,10},{7,3},{... | collective-permute-start | bytes 393224 | tf_op jit(solution)/shard_map/ppermute | solution.py:122
  681.2 68.3 %reduce-scatter.32.cloned.1.call-start = ((), (), s32[]{:S(2)}) async-start(), calls=%async_computation.21 | async-start | bytes 655360 | tf_op jit(solution)/shard_map/reduce_scatter | solution.py:118
  699.6 20.7 %collective-permute-start.52 = (bf16[1,64,4,2,128]{4,1,3,2,0:T(8,128)(2,1)}, bf16[1,64,4,2,128]{4,1,3,2,0:T(8,128)(2,1)S(1)}, u32[]{:S(2)}, u32[]{:S(2)}) collective-permute-start(bf16[1,64,4,2,128]{4,1,3,2,0:T(8,128)(2,1)} %bitcast.495), channel_id=1, source_target_pairs={{4,0},{8,4},{12,8},{5,1},{9,5},{13,9},{6,2},{10,6},{14,10},{7,3},{... | collective-permute-start | bytes 393224 | tf_op jit(solution)/shard_map/ppermute | solution.py:122
  (90 other events, 828.0 us)
Sparse Core Ops, SparseCore 0:
  321.5 20.8 reduce-scatter.11
  356.0 17.1 reduce-scatter.13
  386.9 17.0 reduce-scatter.15
  417.7 17.1 reduce-scatter.17
  448.1 16.9 reduce-scatter.19
  506.9 17.7 reduce-scatter.21
  550.0 17.8 reduce-scatter.23
  593.4 17.8 reduce-scatter.25
  637.3 17.9 reduce-scatter.27
  681.3 18.0 reduce-scatter.29
  724.6 17.9 reduce-scatter.31
